TPU v7x, 32 devices: a whole 2x2x4 slice. The times are simulated.
32 devices in a mesh: grp: 4 (over x, core), tp: 8 (over z, y).
Axes of the slice: x: 2, y: 2, z: 4, core: 2. Of those that a mesh axis runs over, the one named last changes fastest.
Arguments:
- hidden_in: bfloat16 [3072, 3584], P('grp'), may hold values from -6 to 6
- lengths: int32 [8, 8], P('grp'), may hold values from 1 to 96, 384 in all within a row
- dest: int32 [64, 1], P('grp'), may hold values from 0 to 3; in each aligned block of 16 rows (0 to 15, 16 to 31, ...) at most 4 rows name the same one
- attn_gain: float32 [3584], replicated, may hold values from 0.6 to 8
- q_weight: bfloat16 [3584, 2048], P('grp', 'tp'), may hold values from -0.09375 to 0.09375
- k_weight: bfloat16 [3584, 512], P('grp', 'tp'), may hold values from -0.09375 to 0.09375
- v_weight: bfloat16 [3584, 512], P('grp', 'tp'), may hold values from -0.09375 to 0.09375
- o_weight: bfloat16 [3584, 2048], P('grp', 'tp'), may hold values from -0.125 to 0.125
- ffn_gain: float32 [3584], replicated, may hold values from 0.1 to 1.9
- gate_weight: bfloat16 [3584, 10240], P('grp', 'tp'), may hold values from -0.09375 to 0.09375
- up_weight: bfloat16 [3584, 10240], P('grp', 'tp'), may hold values from -0.09375 to 0.09375
- down_weight: bfloat16 [3584, 10240], P('grp', 'tp'), may hold values from -0.0625 to 0.0625
Outputs:
- bank_in: bfloat16 [4, 4, 4, 3584], P('grp', None, None, 'tp')
Inputs may be any that keep to these rules, and one draw needn't show every extreme that they name: Each block's 8 lengths sum to 384. `dest`: among the programs of one index of grp, no bank shard is named by more than 4.
All inputs are finite; a program needn't handle non-finite values.
Results may differ from a plain program's by a relative error of at most 0.015.
The roundings to bfloat16 on the way count: a program that leaves them out, or rounds other values in their place, can miss the bound.
Values may be sent and summed in bfloat16 or wider, within the bound.
No kernel may reach another device: no remote copies, remote signals or barrier semaphores. Data moves between devices by JAX's collectives and lax.ppermute only.
A program may use at most 128 MiB of HBM per device.

v0:
```python
import jax
import jax.numpy as jnp
from jax import lax
from jax.sharding import PartitionSpec as P

HEAD_SIZE = 128
KVH = 4
HEADS = 16
EPSILON = 1e-06
HIGH = lax.Precision.HIGHEST


def rms_scale(rows, gain):
    rows = rows.astype(jnp.float32)
    factor = lax.rsqrt(jnp.mean(rows * rows, axis=1, keepdims=True) + EPSILON)
    return (rows * factor * gain[None, :]).astype(jnp.bfloat16)


def segment_ids(lengths, block_rows):
    bounds = jnp.cumsum(lengths, axis=1)
    position = lax.broadcasted_iota(jnp.int32, (lengths.shape[0], block_rows), 1)
    return jnp.sum((position[:, :, None] >= bounds[:, None, :]).astype(jnp.int32), axis=2)


def softmax_rows(attention_scores):
    top = jnp.max(attention_scores, axis=-1, keepdims=True)
    expo = jnp.exp(attention_scores - top)
    return (expo / jnp.sum(expo, axis=-1, keepdims=True)).astype(jnp.bfloat16)


def transposed_dot(left, right):
    return lax.dot_general(
        left, right, (((1,), (1,)), ((), ())), preferred_element_type=jnp.float32
    )


def gather_grp(piece, chips):
    held = [piece]
    moving = piece
    if chips > 1:
        ring = [(2 * i + c, 2 * ((i + 1) % chips) + c) for i in range(chips) for c in range(2)]
        for _ in range(chips - 1):
            moving = lax.ppermute(moving, "grp", ring)
            held.append(moving)
    mine = jnp.stack(held)
    other = lax.ppermute(mine, "grp", [(g, g ^ 1) for g in range(2 * chips)])
    return jnp.concatenate([mine, other], 0)


def source_order(chips):
    g = lax.axis_index("grp")
    chip, core = (g // 2, g % 2)
    steps = jnp.arange(chips, dtype=jnp.int32)
    own = 2 * ((chip - steps) % chips) + core
    return jnp.concatenate([own, own - core + (1 - core)])


def take_blocks(x, order, size, axis):
    return jnp.concatenate(
        [lax.dynamic_slice_in_dim(x, order[k] * size, size, axis) for k in range(order.shape[0])],
        axis,
    )


def on_device(
    hidden_in,
    lengths,
    dest,
    attn_gain,
    q_weight,
    k_weight,
    v_weight,
    o_weight,
    ffn_gain,
    gate_weight,
    up_weight,
    down_weight,
):
    row_count, width = hidden_in.shape
    blocks, per_block = lengths.shape
    block_rows = row_count // blocks
    programs = blocks * per_block
    tp_size = lax.axis_size("tp")
    grp_size = lax.axis_size("grp")
    chips = grp_size // 2
    tp_index = lax.axis_index("tp")
    grp_index = lax.axis_index("grp")
    d_grp = width // grp_size
    d_tp = width // tp_size
    ratio = tp_size // grp_size
    capacity = max(2, (programs + grp_size - 1) // grp_size)
    local_heads = q_weight.shape[1] // HEAD_SIZE
    order = source_order(chips)
    q_cols, k_cols = (q_weight.shape[1], k_weight.shape[1])
    qkv_full = gather_grp(jnp.concatenate([q_weight, k_weight, v_weight], 1), chips)
    qkv_full = qkv_full.reshape(width, -1)
    o_full = gather_grp(o_weight, chips).reshape(width, -1)
    gate_full = gather_grp(gate_weight, chips).reshape(width, -1)
    up_full = gather_grp(up_weight, chips).reshape(width, -1)
    hidden_perm = take_blocks(hidden_in, order, d_grp, 1)
    attn_gain_perm = take_blocks(attn_gain, order, d_grp, 0)
    ffn_gain_perm = take_blocks(ffn_gain, order, d_grp, 0)
    norm_in = rms_scale(hidden_perm, attn_gain_perm)
    qkv = jnp.dot(norm_in, qkv_full, preferred_element_type=jnp.float32).astype(jnp.bfloat16)
    queries = qkv[:, :q_cols]
    kv_part = qkv[:, q_cols:]
    kv_all = lax.all_to_all(
        jnp.broadcast_to(kv_part[None], (tp_size,) + kv_part.shape), "tp", 0, 0, tiled=True
    )
    per_dev = k_cols // KVH
    kv_index = tp_index * local_heads // (HEADS // KVH)

    def head_of(part):
        split = part.reshape(tp_size, row_count, per_dev, KVH)
        one = lax.dynamic_slice_in_dim(split, kv_index, 1, 3)[..., 0]
        return one.transpose(1, 0, 2).reshape(row_count, tp_size * per_dev)

    key_head = head_of(kv_all[:, :, :k_cols])
    value_head = head_of(kv_all[:, :, k_cols:])
    segs = segment_ids(lengths, block_rows)
    same = segs[:, :, None] == segs[:, None, :]
    blocked_queries = queries.reshape(blocks, block_rows, local_heads, HEAD_SIZE)
    blocked_keys = key_head.reshape(blocks, block_rows, HEAD_SIZE)
    blocked_values = value_head.reshape(blocks, block_rows, HEAD_SIZE)
    attention_scores = jnp.einsum(
        "xwre,xpe->xrwp", blocked_queries, blocked_keys, preferred_element_type=jnp.float32
    ) * HEAD_SIZE ** (-0.5)
    attention_scores = jnp.where(same[:, None, :, :], attention_scores, -1e30)
    attention_probabilities = softmax_rows(attention_scores)
    attended_rows = jnp.einsum(
        "asfo,aon->afsn",
        attention_probabilities,
        blocked_values,
        preferred_element_type=jnp.float32,
    )
    attended_rows = attended_rows.astype(jnp.bfloat16).reshape(row_count, local_heads * HEAD_SIZE)
    attn_term = transposed_dot(attended_rows, o_full)
    attn_total = lax.psum(attn_term.astype(jnp.bfloat16), "tp").astype(jnp.float32)
    residual = hidden_perm.astype(jnp.float32) + attn_total
    norm_mid = rms_scale(residual, ffn_gain_perm)
    gate_pre = jnp.dot(norm_mid, gate_full, preferred_element_type=jnp.float32)
    up_pre = jnp.dot(norm_mid, up_full, preferred_element_type=jnp.float32)
    hidden_ffn = (jax.nn.silu(gate_pre) * up_pre).astype(jnp.bfloat16)
    block_index = lax.broadcasted_iota(jnp.int32, (blocks, block_rows), 0)
    program_of_row = (block_index * per_block + segs).reshape(row_count)
    program_grid = lax.broadcasted_iota(jnp.int32, (programs, row_count), 0)
    selector = (program_grid == program_of_row[None, :]).astype(jnp.float32)
    hidden_sums = jnp.dot(
        selector.astype(jnp.bfloat16), hidden_ffn, preferred_element_type=jnp.float32
    )
    chunk_owner = tp_index // ratio
    owner_step = jnp.argmax(order == chunk_owner).astype(jnp.int32)
    chunk_start = owner_step * d_grp + tp_index % ratio * d_tp
    residual_chunk = lax.dynamic_slice_in_dim(residual, chunk_start, d_tp, 1)
    residual_sums = jnp.dot(
        selector, residual_chunk, precision=HIGH, preferred_element_type=jnp.float32
    )
    hidden_all = gather_grp(hidden_sums, chips).reshape(grp_size * programs, -1)
    down_part = lax.dot_general(
        hidden_all,
        down_weight.astype(jnp.float32),
        (((1,), (1,)), ((), ())),
        precision=HIGH,
        preferred_element_type=jnp.float32,
    )
    dest_all = gather_grp(dest[:, 0], chips)
    lengths_all = gather_grp(lengths.reshape(programs), chips).reshape(grp_size * programs)
    grp_ids = lax.broadcasted_iota(jnp.int32, (grp_size, programs, grp_size), 2)
    chosen = (dest_all[:, :, None] == grp_ids).astype(jnp.int32)
    earlier = jnp.cumsum(chosen, axis=1) - chosen
    slot_rank = jnp.sum(earlier * chosen, axis=2)
    slot_row = order[:, None] * capacity + slot_rank
    slots = grp_size * capacity
    target_grid = lax.broadcasted_iota(jnp.int32, (grp_size, slots, grp_size, programs), 0)
    row_grid = lax.broadcasted_iota(jnp.int32, (grp_size, slots, grp_size, programs), 1)
    placer = (
        ((target_grid == dest_all[None, None]) & (row_grid == slot_row[None, None]))
        .astype(jnp.float32)
        .reshape(grp_size, slots, grp_size * programs)
    )
    down_slots = jnp.einsum("asq,qd->asd", placer, down_part, precision=HIGH)
    down_slots = down_slots.reshape(grp_size, slots, ratio, d_tp).transpose(0, 2, 1, 3)
    send = lax.dynamic_update_slice(
        jnp.zeros((grp_size, tp_size, slots, d_tp), jnp.float32),
        down_slots,
        (0, grp_index * ratio, 0, 0),
    )
    local_placer = placer[:, :, :programs]
    residual_slots = jnp.einsum("asq,qd->asd", local_placer, residual_sums, precision=HIGH)
    send = send + lax.dynamic_update_slice(
        jnp.zeros((grp_size, tp_size, slots, d_tp), jnp.float32),
        residual_slots[:, None],
        (0, tp_index, 0, 0),
    )
    received = lax.all_to_all(
        send.reshape(grp_size * tp_size, slots, d_tp), ("grp", "tp"), 0, 0, tiled=True
    )
    totals = jnp.sum(received, axis=0)
    mine = lax.dynamic_index_in_dim(placer, grp_index, 0, keepdims=False)
    counts = jnp.dot(mine, lengths_all.astype(jnp.float32), precision=HIGH)
    counts = jnp.where(counts > 0, counts, 1.0)
    embedded = (totals / counts[:, None]).astype(jnp.bfloat16)
    return embedded.reshape(1, grp_size, capacity, d_tp)


def solution(mesh):
    placed = (
        P("grp", None),
        P("grp", None),
        P("grp", None),
        P(),
        P("grp", "tp"),
        P("grp", "tp"),
        P("grp", "tp"),
        P("grp", "tp"),
        P(),
        P("grp", "tp"),
        P("grp", "tp"),
        P("grp", "tp"),
    )
    return jax.shard_map(
        on_device, mesh=mesh, in_specs=placed, out_specs=P("grp", None, None, "tp"), check_vma=False
    )
```

profile of v0, /device:TPU:0, one launch (start us, length us, event | category | flops | bytes accessed | tf_op | source)
XLA Modules:
  0.0 450.6 jit_solution(4661509185440796981)
XLA Ops:
  8.8 2.0 pad_maximum_fusion.9
  10.9 2.9 collective-permute-start.2
  16.9 13.5 %collective-permute-done.2 = bf16[896,384]{1,0:T(8,128)(2,1)} collective-permute-done((bf16[896,384]{1,0:T(8,128)(2,1)}, bf16[896,384]{1,0:T(8,128)(2,1)}, u32[]{:S(2)}, u32[]{:S(2)}) %collective-permute-start.2) | collective-permute-done | bytes 688160 | tf_op jit(solution)/shard_map/ppermute | solution.py:43
  30.4 2.4 pad_maximum_fusion.7
  34.7 3.1 constant_dynamic-slice_fusion.5
  37.8 1.4 fusion.1
  39.2 2.3 pad_maximum_fusion.5
  41.5 4.1 fusion.12
  47.8 6.4 %all-to-all-start = ((bf16[8,768,128]{1,2,0:T(8,128)(2,1)}), bf16[8,768,128]{1,2,0:T(8,128)(2,1)}, u32[]{:S(2)}, u32[]{:S(2)}) async-start(bf16[8,768,128]{1,2,0:T(8,128)(2,1)} %broadcast_in_dim.19), calls=%async_computation | async-start | bytes 3145728 | tf_op jit(solution)/shard_map/all_to_all | solution.py:107
  54.3 1.5 collective-permute-start.8
  56.4 81.2 %collective-permute-done.4 = bf16[896,256]{1,0:T(8,128)(2,1)S(1)} collective-permute-done((bf16[896,256]{1,0:T(8,128)(2,1)S(1)}, bf16[896,256]{1,0:T(8,128)(2,1)S(1)}, u32[]{:S(2)}, u32[]{:S(2)}) %collective-permute-start.4) | collective-permute-done | bytes 458784 | tf_op jit(solution)/shard_map/ppermute | solution.py:43
  139.8 1.6 collective-permute-done.5
  141.4 2.6 pad_maximum_fusion.6
  145.9 5.1 %pad_maximum_fusion.3 = bf16[2,896,1280]{2,1,0:T(8,128)(2,1)} fusion(bf16[1,896,1280]{2,1,0:T(8,128)(2,1)} %bitcast.25, bf16[1,896,1280]{2,1,0:T(8,128)(2,1)} %bitcast.96), kind=kLoop, calls=%fused_computation.16 | loop fusion | flops 2293760 | bytes 9175040 | tf_op jit(solution)/shard_map/stack | solution.py:45
  151.1 4.1 pad_maximum_fusion.4
  155.6 1.5 fusion.58
  158.3 3.5 fusion.63
  161.8 2.0 fusion.15
  164.4 5.6 %convolution_convert_fusion = bf16[768,3584]{1,0:T(8,128)(2,1)} fusion(bf16[3584,256]{1,0:T(8,128)(2,1)} %bitcast.102, bf16[96,8,2,128]{3,2,1,0:T(2,128)(2,1)S(1)} %bitcast.105), kind=kOutput, calls=%fused_computation.11 | convolution fusion | flops 1412038656 | bytes 7733248 | tf_op jit(solution)/shard_map/dot_general | solution.py:32
  170.1 1.7 collective-permute-start.12
  177.0 9.9 %pad_maximum_fusion = bf16[4,896,1280]{2,1,0:T(8,128)(2,1)} fusion(bf16[2,896,1280]{2,1,0:T(8,128)(2,1)} %collective-permute-done.7, bf16[1,896,1280]{2,1,0:T(8,128)(2,1)} %bitcast.25, bf16[1,896,1280]{2,1,0:T(8,128)(2,1)} %bitcast.97), kind=kLoop, calls=%fused_computation.9 | loop fusion | flops 9175040 | bytes 18350080 | tf_op jit(solution)/shard_map/concatenate | solution.py:47
  186.9 8.2 %pad_maximum_fusion.1 = bf16[4,896,1280]{2,1,0:T(8,128)(2,1)} fusion(bf16[2,896,1280]{2,1,0:T(8,128)(2,1)} %collective-permute-done.9, bf16[1,896,1280]{2,1,0:T(8,128)(2,1)} %bitcast.28, bf16[1,896,1280]{2,1,0:T(8,128)(2,1)S(1)} %bitcast.99), kind=kLoop, calls=%fused_computation.10 | loop fusion | flops 9175040 | bytes 18350080 | tf_op jit(solution)/shard_map/concatenate | solution.py:47
  195.1 167.2 %all-reduce.2.cloned.1.call-done = bf16[768,3584]{1,0:T(8,128)(2,1)} async-done(((bf16[768,3584]{1,0:T(8,128)(2,1)}), bf16[768,3584]{1,0:T(8,128)(2,1)}) %all-reduce.2.cloned.1.call-update) | async-done | bytes 5505040 | tf_op jit(solution)/shard_map/psum | solution.py:138
  362.4 11.9 %convert_add_fusion = (f32[768,3584]{1,0:T(8,128)}, f32[768]{0:T(1024)S(1)}) fusion(bf16[768,3584]{1,0:T(8,128)(2,1)} %all-reduce.2.cloned.1.call-done, bf16[768,896]{1,0:T(8,128)(2,1)} %copy-done.5, bf16[768,896]{1,0:T(8,128)(2,1)} %copy-done.7, bf16[768,896]{1,0:T(8,128)(2,1)} %copy-done.3, bf16[768,896]{1,0:T(8,128)(2,1)} %copy-done.1), kind=kLoop, calls=%fused_computation.1 | loop fusion | flops 33029376 | bytes 22023168 | tf_op jit(solution)/shard_map/add | solution.py:139
  374.3 11.6 %fusion.56 = f32[768,1280]{1,0:T(8,128)} fusion(bf16[3584,1280]{1,0:T(8,128)(2,1)S(1)} %bitcast.101, f32[3584]{0:T(1024)S(1)} %pad_maximum_fusion.13, f32[768]{0:T(1024)S(1)} %add_rsqrt_fusion, bf16[768,3584]{1,0:T(8,128)(2,1)} %all-reduce.2.cloned.1.call-done, bf16[768,896]{1,0:T(8,128)(2,1)S(1)} %copy-done.6, bf16[768,896]{1,0:T(8,128)(2,1)S(1)} %copy-done.8, ...), kind=kOutput, calls=%fused_computation.111 | convolution fusion | flops 7082213376 | bytes 24134656 | tf_op jit(solution)/shard_map/dot_general | solution.py:142
  386.0 14.4 %fusion.9 = f32[16,1280]{1,0:T(8,128)S(1)} fusion(f32[768,1280]{1,0:T(8,128)} %fusion.56, s32[768]{0:T(1024)S(1)} %add.143, bf16[3584,1280]{1,0:T(8,128)(2,1)} %bitcast.100, f32[3584]{0:T(1024)S(1)} %pad_maximum_fusion.13, f32[768]{0:T(1024)S(1)} %add_rsqrt_fusion, bf16[768,3584]{1,0:T(8,128)(2,1)} %all-reduce.2.cloned.1.call-done, ...), kind=kOutput, calls=%fused_computation.24 | convolution fusion | flops 7119605760 | bytes 24219648 | tf_op jit(solution)/shard_map/dot_general | solution.py:148
  400.4 1.5 collective-permute-start.10
  402.2 2.8 collective-permute-done.10
  405.2 2.3 fusion.21
  407.6 2.1 convolution_bitcast_fusion.1
  411.7 3.7 all-to-all-start.1
  416.9 26.1 %all-to-all-done.1 = f32[32,16,448]{2,1,0:T(8,128)S(1)} async-done(((f32[32,16,448]{2,1,0:T(8,128)}), f32[32,16,448]{2,1,0:T(8,128)S(1)}, u32[]{:S(2)}, u32[]{:S(2)}) %all-to-all-start.1) | async-done | bytes 917536 | tf_op jit(solution)/shard_map/all_to_all | solution.py:195
  (125 shorter events, 23.3 us)
Async XLA Ops:
  6.5 401.0 %copy-start = (bf16[896,1280]{1,0:T(8,128)(2,1)S(1)}, bf16[896,1280]{1,0:T(8,128)(2,1)}, u32[]{:S(2)}) copy-start(bf16[896,1280]{1,0:T(8,128)(2,1)} %param.23) | copy-start | bytes 6881284
  6.5 28.0 %copy-start.14 = (f32[3584]{0:T(1024)S(1)}, f32[3584]{0:T(1024)}, u32[]{:S(2)}) copy-start(f32[3584]{0:T(1024)} %param.15) | copy-start | bytes 43012
  10.9 19.5 %collective-permute-start.2 = (bf16[896,384]{1,0:T(8,128)(2,1)}, bf16[896,384]{1,0:T(8,128)(2,1)}, u32[]{:S(2)}, u32[]{:S(2)}) collective-permute-start(bf16[896,384]{1,0:T(8,128)(2,1)} %pad_maximum_fusion.9), channel_id=1, source_target_pairs={{0,16},{8,24},{16,0},{24,8},{1,17},{9,25},{17,1},{25,9},{2,18},{10... | collective-permute-start | bytes 2064392 | tf_op jit(solution)/shard_map/ppermute | solution.py:43
  13.8 132.1 %collective-permute-start.6 = (bf16[896,1280]{1,0:T(8,128)(2,1)}, bf16[896,1280]{1,0:T(8,128)(2,1)}, u32[]{:S(2)}, u32[]{:S(2)}) collective-permute-start(bf16[896,1280]{1,0:T(8,128)(2,1)} %param.21), channel_id=1, source_target_pairs={{0,16},{8,24},{16,0},{24,8},{1,17},{9,25},{17,1},{25,9},{2,18},{10... | collective-permute-start | bytes 6881288 | tf_op jit(solution)/shard_map/ppermute | solution.py:43
  32.7 6.4 %collective-permute-start.3 = (bf16[2,896,384]{2,1,0:T(8,128)(2,1)}, bf16[2,896,384]{2,1,0:T(8,128)(2,1)}, u32[]{:S(2)}, u32[]{:S(2)}) collective-permute-start(bf16[2,896,384]{2,1,0:T(8,128)(2,1)} %pad_maximum_fusion.7), channel_id=1, source_target_pairs={{0,8},{8,0},{16,24},{24,16},{1,9},{9,1},{17,25},{25,17},{2,10},{10... | collective-permute-start | bytes 4128776 | tf_op jit(solution)/shard_map/ppermute | solution.py:46
  37.7 3.7 copy-start.1
  37.7 3.7 copy-start.3
  37.7 3.7 copy-start.5
  46.4 9.4 %copy-start.12 = (bf16[896,256]{1,0:T(8,128)(2,1)S(1)}, bf16[896,256]{1,0:T(8,128)(2,1)}, u32[]{:S(2)}) copy-start(bf16[896,256]{1,0:T(8,128)(2,1)} %param.19) | copy-start | bytes 1376260
  46.4 92.2 %copy-start.17 = (s32[2,8]{1,0:T(2,128)S(1)}, s32[2,8]{1,0:T(2,128)}, u32[]{:S(2)}) copy-start(s32[2,8]{1,0:T(2,128)} %param.13) | copy-start | bytes 196
  47.8 107.8 %all-to-all-start = ((bf16[8,768,128]{1,2,0:T(8,128)(2,1)}), bf16[8,768,128]{1,2,0:T(8,128)(2,1)}, u32[]{:S(2)}, u32[]{:S(2)}) async-start(bf16[8,768,128]{1,2,0:T(8,128)(2,1)} %broadcast_in_dim.19), calls=%async_computation | async-start | bytes 3145728 | tf_op jit(solution)/shard_map/all_to_all | solution.py:107
  54.3 308.1 %all-reduce.2.cloned.1.call-start = ((), (), s32[]{:S(2)}) async-start(), calls=%async_computation.2 | async-start | bytes 11010048 | tf_op jit(solution)/shard_map/psum | solution.py:138
  54.3 96.8 %collective-permute-start.8 = (bf16[896,1280]{1,0:T(8,128)(2,1)}, bf16[896,1280]{1,0:T(8,128)(2,1)}, u32[]{:S(2)}, u32[]{:S(2)}) collective-permute-start(bf16[896,1280]{1,0:T(8,128)(2,1)} %param.22), channel_id=1, source_target_pairs={{0,16},{8,24},{16,0},{24,8},{1,17},{9,25},{17,1},{25,9},{2,18},{10... | collective-permute-start | bytes 6881288 | tf_op jit(solution)/shard_map/ppermute | solution.py:43
  55.8 81.7 %collective-permute-start.4 = (bf16[896,256]{1,0:T(8,128)(2,1)S(1)}, bf16[896,256]{1,0:T(8,128)(2,1)S(1)}, u32[]{:S(2)}, u32[]{:S(2)}) collective-permute-start(bf16[896,256]{1,0:T(8,128)(2,1)S(1)} %copy-done.12), channel_id=1, source_target_pairs={{0,16},{8,24},{16,0},{24,8},{1,17},{9,25},{17,1},{25,9},{2,18},{10... | collective-permute-start | bytes 1376264 | tf_op jit(solution)/shard_map/ppermute | solution.py:43
  138.6 2.8 collective-permute-start.5
  145.9 5.2 %copy-start.9 = (bf16[896,1280]{1,0:T(8,128)(2,1)S(1)}, bf16[896,1280]{1,0:T(8,128)(2,1)}, u32[]{:S(2)}) copy-start(bf16[896,1280]{1,0:T(8,128)(2,1)} %param.22) | copy-start | bytes 6881284
  151.0 26.0 %collective-permute-start.7 = (bf16[2,896,1280]{2,1,0:T(8,128)(2,1)}, bf16[2,896,1280]{2,1,0:T(8,128)(2,1)}, u32[]{:S(2)}, u32[]{:S(2)}) collective-permute-start(bf16[2,896,1280]{2,1,0:T(8,128)(2,1)} %pad_maximum_fusion.3), channel_id=1, source_target_pairs={{0,8},{8,0},{16,24},{24,16},{1,9},{9,1},{17,25},{25,17},{2,10},{10... | collective-permute-start | bytes 13762568 | tf_op jit(solution)/shard_map/ppermute | solution.py:46
  155.2 31.7 %collective-permute-start.9 = (bf16[2,896,1280]{2,1,0:T(8,128)(2,1)}, bf16[2,896,1280]{2,1,0:T(8,128)(2,1)}, u32[]{:S(2)}, u32[]{:S(2)}) collective-permute-start(bf16[2,896,1280]{2,1,0:T(8,128)(2,1)} %pad_maximum_fusion.4), channel_id=1, source_target_pairs={{0,8},{8,0},{16,24},{24,16},{1,9},{9,1},{17,25},{25,17},{2,10},{10... | collective-permute-start | bytes 13762568 | tf_op jit(solution)/shard_map/ppermute | solution.py:46
  170.0 4.2 copy-start.15
  170.1 4.3 collective-permute-start.12
  171.9 3.5 collective-permute-start
  175.4 1.2 collective-permute-start.1
  177.0 9.9 %copy-start.10 = (bf16[896,1280]{1,0:T(8,128)(2,1)S(1)}, bf16[896,1280]{1,0:T(8,128)(2,1)}, u32[]{:S(2)}) copy-start(bf16[896,1280]{1,0:T(8,128)(2,1)} %param.22) | copy-start | bytes 6881284
  362.4 11.9 %copy-start.2 = (bf16[768,896]{1,0:T(8,128)(2,1)S(1)}, bf16[768,896]{1,0:T(8,128)(2,1)}, u32[]{:S(2)}) copy-start(bf16[768,896]{1,0:T(8,128)(2,1)} %copy-done.1) | copy-start | bytes 4128772
  362.4 11.9 %copy-start.4 = (bf16[768,896]{1,0:T(8,128)(2,1)S(1)}, bf16[768,896]{1,0:T(8,128)(2,1)}, u32[]{:S(2)}) copy-start(bf16[768,896]{1,0:T(8,128)(2,1)} %copy-done.3) | copy-start | bytes 4128772
  362.4 11.9 %copy-start.6 = (bf16[768,896]{1,0:T(8,128)(2,1)S(1)}, bf16[768,896]{1,0:T(8,128)(2,1)}, u32[]{:S(2)}) copy-start(bf16[768,896]{1,0:T(8,128)(2,1)} %copy-done.5) | copy-start | bytes 4128772
  362.4 11.9 %copy-start.8 = (bf16[768,896]{1,0:T(8,128)(2,1)S(1)}, bf16[768,896]{1,0:T(8,128)(2,1)}, u32[]{:S(2)}) copy-start(bf16[768,896]{1,0:T(8,128)(2,1)} %copy-done.7) | copy-start | bytes 4128772
  362.4 11.9 %copy-start.11 = (bf16[4,896,1280]{2,1,0:T(8,128)(2,1)S(1)}, bf16[4,896,1280]{2,1,0:T(8,128)(2,1)}, u32[]{:S(2)}) copy-start(bf16[4,896,1280]{2,1,0:T(8,128)(2,1)} %pad_maximum_fusion.1) | copy-start | bytes 27525124
  400.4 4.5 %collective-permute-start.10 = (f32[16,1280]{1,0:T(8,128)S(1)}, f32[16,1280]{1,0:T(8,128)S(1)}, u32[]{:S(2)}, u32[]{:S(2)}) collective-permute-start(f32[16,1280]{1,0:T(8,128)S(1)} %fusion.9), channel_id=1, source_target_pairs={{0,16},{8,24},{16,0},{24,8},{1,17},{9,25},{17,1},{25,9},{2,18},{10... | collective-permute-start | bytes 245768 | tf_op jit(solution)/shard_map/ppermute | solution.py:43
  404.9 2.6 collective-permute-start.11
  411.7 31.3 %all-to-all-start.1 = ((f32[32,16,448]{2,1,0:T(8,128)}), f32[32,16,448]{2,1,0:T(8,128)S(1)}, u32[]{:S(2)}, u32[]{:S(2)}) async-start(f32[32,16,448]{2,1,0:T(8,128)} %bitcast.103), calls=%async_computation.1 | async-start | bytes 2097152 | tf_op jit(solution)/shard_map/all_to_all | solution.py:195
  415.4 1.2 collective-permute-start.13
  (3 other events, 6.4 us)
Sparse Core Ops, SparseCore 0:
  170.2 192.1 all-reduce.1
where the time goes:
time: 452 us; the launch traced here: 451 us
  waiting for transfers between devices  295 us (65%)
  other arithmetic  55.5 us (12%)
  matrix products  46.4 us (10%)
  starting transfers between devices  20 us (4%)
  between operations  17 us (4%)
  local copies, waits for them, and re-layouts  16.4 us (4%)
    psum x1, waiting for transfers between devices, on_device(): lax.psum(attn_term.astype(jnp.bfloat16), 'tp').astype(jnp.float32)  167 us
    ppermute x7, waiting for transfers between devices, gather_grp(): moving = lax.ppermute(moving, 'grp', ring)  98.4 us
    all_to_all x1, waiting for transfers between devices, on_device(): lax.all_to_all(send.reshape(grp_size * tp_size, slots, d_tp), ('grp', 'tp...  26.1 us
    concatenate x6, other arithmetic, gather_grp(): return jnp.concatenate([mine, other], 0)  23 us
    dot_general x1, matrix products, on_device(): jnp.dot(selector.astype(jnp.bfloat16), hidden_ffn, preferred_element_type...  14.4 us
    another operation x7, other arithmetic, gather_grp(): mine = jnp.stack(held)  13.7 us
    add x1, other arithmetic, on_device(): residual = hidden_perm.astype(jnp.float32) + attn_total  11.9 us
    dot_general x1, matrix products, on_device(): up_pre = jnp.dot(norm_mid, up_full, preferred_element_type=jnp.float32)  11.6 us
  transfers between devices with their start and end apart: 17, of which 9 were waited for; matrix products, arithmetic and copies ran while one was open for 16% of the time, Pallas kernels for 0%

commit v1 on v0

--- a/solution.py
+++ b/solution.py
@@ -8,6 +8,12 @@
 HEADS = 16
 EPSILON = 1e-06
 HIGH = lax.Precision.HIGHEST
+
+
+def add_all(x, mesh_axis):
+    shards = lax.all_gather(x, mesh_axis, axis=0, tiled=False)
+    result = shards.sum(axis=0)
+    return result
 
 
 def rms_scale(rows, gain):
@@ -135,7 +141,7 @@
     )
     attended_rows = attended_rows.astype(jnp.bfloat16).reshape(row_count, local_heads * HEAD_SIZE)
     attn_term = transposed_dot(attended_rows, o_full)
-    attn_total = lax.psum(attn_term.astype(jnp.bfloat16), "tp").astype(jnp.float32)
+    attn_total = add_all(attn_term.astype(jnp.bfloat16), "tp").astype(jnp.float32)
     residual = hidden_perm.astype(jnp.float32) + attn_total
     norm_mid = rms_scale(residual, ffn_gain_perm)
     gate_pre = jnp.dot(norm_mid, gate_full, preferred_element_type=jnp.float32)

time: 452 us -> 1050 us (2.32)
  waiting for transfers between devices: 295 us -> 874 us
  other arithmetic: 55.5 us -> 70.7 us
    all_gather x0 -> x1, waiting for transfers between devices: none -> 705 us  [add_all(): shards = lax.all_gather(x, mesh_axis, axis=0, tiled=False)]
    psum x1 -> x0, waiting for transfers between devices: 167 us -> none  [on_device(): lax.psum(attn_term.astype(jnp.bfloat16), 'tp').astype(jnp.float32)]
    ppermute x7, waiting for transfers between devices: 98.4 us -> 121 us  [gather_grp(): moving = lax.ppermute(moving, 'grp', ring)]
    reduce_sum x0 -> x1, other arithmetic: none -> 18.1 us  [add_all(): result = shards.sum(axis=0)]
    all_to_all x1, waiting for transfers between devices: 0.01 us -> 16.5 us  [on_device(): lax.all_to_all(jnp.broadcast_to(kv_part[None], (tp_size,) + kv_part.shape...]
  transfers between devices with their start and end apart: 17 -> 17, of which waited for: 9 -> 12; matrix products, arithmetic and copies ran while one was open for 16% -> 4% of each run, Pallas kernels for 0% -> 0%
where the time goes in v1:
time: 1050 us
  waiting for transfers between devices  874 us (83%)
  other arithmetic  70.7 us (7%)
  matrix products  48.3 us (5%)
  starting transfers between devices  21.6 us (2%)
  between operations  17 us (2%)
  local copies, waits for them, and re-layouts  16.2 us (2%)
    all_gather x1, waiting for transfers between devices, add_all(): shards = lax.all_gather(x, mesh_axis, axis=0, tiled=False)  705 us
    ppermute x7, waiting for transfers between devices, gather_grp(): moving = lax.ppermute(moving, 'grp', ring)  121 us
    all_to_all x1, waiting for transfers between devices, on_device(): lax.all_to_all(send.reshape(grp_size * tp_size, slots, d_tp), ('grp', 'tp...  26.1 us
    concatenate x6, other arithmetic, gather_grp(): return jnp.concatenate([mine, other], 0)  22.1 us
  transfers between devices with their start and end apart: 17, of which 12 were waited for; matrix products, arithmetic and copies ran while one was open for 4% of the time, Pallas kernels for 0%

profile of v1, /device:TPU:0, one launch (start us, length us, event | category | flops | bytes accessed | tf_op | source)
XLA Modules:
  0.0 1047.4 jit_solution(4563804473616701375)
XLA Ops:
  8.8 2.0 pad_maximum_fusion.9
  10.9 2.9 collective-permute-start.2
  16.8 12.8 %collective-permute-done.2 = bf16[896,384]{1,0:T(8,128)(2,1)} collective-permute-done((bf16[896,384]{1,0:T(8,128)(2,1)}, bf16[896,384]{1,0:T(8,128)(2,1)}, u32[]{:S(2)}, u32[]{:S(2)}) %collective-permute-start.2) | collective-permute-done | bytes 688160 | tf_op jit(solution)/shard_map/ppermute | solution.py:49
  29.5 2.3 pad_maximum_fusion.7
  33.9 3.1 constant_dynamic-slice_fusion.5
  38.4 2.3 pad_maximum_fusion.5
  40.7 4.1 fusion.12
  47.1 6.1 all-to-all-start
  54.9 11.1 %collective-permute-done.4 = bf16[896,256]{1,0:T(8,128)(2,1)S(1)} collective-permute-done((bf16[896,256]{1,0:T(8,128)(2,1)S(1)}, bf16[896,256]{1,0:T(8,128)(2,1)S(1)}, u32[]{:S(2)}, u32[]{:S(2)}) %collective-permute-start.4) | collective-permute-done | bytes 458784 | tf_op jit(solution)/shard_map/ppermute | solution.py:49
  68.3 1.6 collective-permute-done.5
  69.9 2.6 pad_maximum_fusion.6
  74.4 16.5 %all-to-all-done = bf16[8,768,128]{1,2,0:T(8,128)(2,1)} async-done(((bf16[8,768,128]{1,2,0:T(8,128)(2,1)}), bf16[8,768,128]{1,2,0:T(8,128)(2,1)}, u32[]{:S(2)}, u32[]{:S(2)}) %all-to-all-start) | async-done | bytes 1572896 | tf_op jit(solution)/shard_map/all_to_all | solution.py:113
  93.6 3.5 fusion.63
  97.1 2.0 fusion.15
  99.5 5.5 convolution_convert_fusion
  107.1 51.0 %collective-permute-done.8 = bf16[896,1280]{1,0:T(8,128)(2,1)S(1)} collective-permute-done((bf16[896,1280]{1,0:T(8,128)(2,1)}, bf16[896,1280]{1,0:T(8,128)(2,1)S(1)}, u32[]{:S(2)}, u32[]{:S(2)}) %collective-permute-start.8) | collective-permute-done | bytes 2293792 | tf_op jit(solution)/shard_map/ppermute | solution.py:49
  158.1 5.1 pad_maximum_fusion.4
  163.3 42.4 %collective-permute-done.6 = bf16[896,1280]{1,0:T(8,128)(2,1)S(1)} collective-permute-done((bf16[896,1280]{1,0:T(8,128)(2,1)}, bf16[896,1280]{1,0:T(8,128)(2,1)S(1)}, u32[]{:S(2)}, u32[]{:S(2)}) %collective-permute-start.6) | collective-permute-done | bytes 2293792 | tf_op jit(solution)/shard_map/ppermute | solution.py:49
  205.6 2.8 pad_maximum_fusion.3
  213.8 2.4 collective-permute-done.1
  216.6 10.2 pad_maximum_fusion.1
  226.7 7.0 pad_maximum_fusion
  233.7 704.9 %all-gather.3.cloned.1.call-done = bf16[6144,3584]{1,0:T(8,128)(2,1)} async-done(((bf16[768,3584]{1,0:T(8,128)(2,1)}), bf16[6144,3584]{1,0:T(8,128)(2,1)}) %all-gather.3.cloned.1.call-update) | async-done | bytes 44040208 | tf_op jit(solution)/shard_map/all_gather | solution.py:14
  938.6 18.1 %reduce_sum.74 = bf16[768,3584]{1,0:T(8,128)(2,1)} reduce(bf16[8,768,3584]{2,1,0:T(8,128)(2,1)} %bitcast.97, bf16[]{:T(256)} %constant.113.clone.1), dimensions={0}, to_apply=%region_7.8 | reduce | flops 19267584 | bytes 49545216 | tf_op jit(solution)/shard_map/reduce_sum | solution.py:15
  956.8 11.3 %convert_add_fusion = (f32[768,3584]{1,0:T(8,128)}, f32[768]{0:T(1024)S(1)}) fusion(bf16[768,3584]{1,0:T(8,128)(2,1)} %reduce_sum.74, bf16[768,896]{1,0:T(8,128)(2,1)} %copy-done.6, bf16[768,896]{1,0:T(8,128)(2,1)} %copy-done.8, bf16[768,896]{1,0:T(8,128)(2,1)} %copy-done.4, bf16[768,896]{1,0:T(8,128)(2,1)} %copy-done.2), kind=kLoop, calls=%fused_computation.1 | loop fusion | flops 33029376 | bytes 22023168 | tf_op jit(solution)/shard_map/add | solution.py:145
  968.1 13.6 %fusion.56 = f32[768,1280]{1,0:T(8,128)} fusion(bf16[3584,1280]{1,0:T(8,128)(2,1)} %bitcast.106, f32[3584]{0:T(1024)S(1)} %pad_maximum_fusion.13, f32[768]{0:T(1024)S(1)} %add_rsqrt_fusion, bf16[768,3584]{1,0:T(8,128)(2,1)S(1)} %copy-done.1, bf16[768,896]{1,0:T(8,128)(2,1)S(1)} %copy-done.7, bf16[768,896]{1,0:T(8,128)(2,1)S(1)} %copy-done.9, ...), kind=kOutput, calls=%fused_computation.111 | convolution fusion | flops 7082213376 | bytes 24134656 | tf_op jit(solution)/shard_map/dot_general | solution.py:148
  981.7 14.5 %fusion.9 = f32[16,1280]{1,0:T(8,128)S(1)} fusion(f32[768,1280]{1,0:T(8,128)} %fusion.56, s32[768]{0:T(1024)S(1)} %add.141, bf16[3584,1280]{1,0:T(8,128)(2,1)} %bitcast.107, f32[3584]{0:T(1024)S(1)} %pad_maximum_fusion.13, f32[768]{0:T(1024)S(1)} %add_rsqrt_fusion, bf16[768,3584]{1,0:T(8,128)(2,1)} %reduce_sum.74, bf16[768,896]{1,0:T(8,128)(2,1)} %copy-done.6, ...), kind=kOutput, calls=%fused_computation.24 | convolution fusion | flops 7119605760 | bytes 24219648 | tf_op jit(solution)/shard_map/dot_general | solution.py:154
  997.9 2.8 collective-permute-done.10
  1000.9 2.3 fusion.21
  1003.3 2.1 convolution_bitcast_fusion.1
  1007.5 4.7 all-to-all-start.1
  1013.7 26.1 %all-to-all-done.1 = f32[32,16,448]{2,1,0:T(8,128)S(1)} async-done(((f32[32,16,448]{2,1,0:T(8,128)}), f32[32,16,448]{2,1,0:T(8,128)S(1)}, u32[]{:S(2)}, u32[]{:S(2)}) %all-to-all-start.1) | async-done | bytes 917536 | tf_op jit(solution)/shard_map/all_to_all | solution.py:201
  (132 shorter events, 30.7 us)
Async XLA Ops:
  6.5 996.8 %copy-start = (bf16[896,1280]{1,0:T(8,128)(2,1)S(1)}, bf16[896,1280]{1,0:T(8,128)(2,1)}, u32[]{:S(2)}) copy-start(bf16[896,1280]{1,0:T(8,128)(2,1)} %param.23) | copy-start | bytes 6881284
  6.5 27.2 %copy-start.17 = (f32[3584]{0:T(1024)S(1)}, f32[3584]{0:T(1024)}, u32[]{:S(2)}) copy-start(f32[3584]{0:T(1024)} %param.15) | copy-start | bytes 43012
  10.9 18.7 %collective-permute-start.2 = (bf16[896,384]{1,0:T(8,128)(2,1)}, bf16[896,384]{1,0:T(8,128)(2,1)}, u32[]{:S(2)}, u32[]{:S(2)}) collective-permute-start(bf16[896,384]{1,0:T(8,128)(2,1)} %pad_maximum_fusion.9), channel_id=1, source_target_pairs={{0,16},{8,24},{16,0},{24,8},{1,17},{9,25},{17,1},{25,9},{2,18},{10... | collective-permute-start | bytes 2064392 | tf_op jit(solution)/shard_map/ppermute | solution.py:49
  31.9 6.5 collective-permute-start.3
  45.6 7.8 copy-start.15
  45.6 21.5 %copy-start.20 = (s32[2,8]{1,0:T(2,128)S(1)}, s32[2,8]{1,0:T(2,128)}, u32[]{:S(2)}) copy-start(s32[2,8]{1,0:T(2,128)} %param.13) | copy-start | bytes 196
  47.1 43.9 %all-to-all-start = ((bf16[8,768,128]{1,2,0:T(8,128)(2,1)}), bf16[8,768,128]{1,2,0:T(8,128)(2,1)}, u32[]{:S(2)}, u32[]{:S(2)}) async-start(bf16[8,768,128]{1,2,0:T(8,128)(2,1)} %broadcast_in_dim.19), calls=%async_computation | async-start | bytes 3145728 | tf_op jit(solution)/shard_map/all_to_all | solution.py:113
  53.2 885.5 %all-gather.3.cloned.1.call-start = ((), (), s32[]{:S(2)}) async-start(), calls=%async_computation.2 | async-start | bytes 49545216 | tf_op jit(solution)/shard_map/all_gather | solution.py:14
  53.4 12.7 %collective-permute-start.4 = (bf16[896,256]{1,0:T(8,128)(2,1)S(1)}, bf16[896,256]{1,0:T(8,128)(2,1)S(1)}, u32[]{:S(2)}, u32[]{:S(2)}) collective-permute-start(bf16[896,256]{1,0:T(8,128)(2,1)S(1)} %copy-done.15), channel_id=1, source_target_pairs={{0,16},{8,24},{16,0},{24,8},{1,17},{9,25},{17,1},{25,9},{2,18},{10... | collective-permute-start | bytes 1376264 | tf_op jit(solution)/shard_map/ppermute | solution.py:49
  67.1 2.8 collective-permute-start.5
  105.1 53.1 %collective-permute-start.8 = (bf16[896,1280]{1,0:T(8,128)(2,1)}, bf16[896,1280]{1,0:T(8,128)(2,1)S(1)}, u32[]{:S(2)}, u32[]{:S(2)}) collective-permute-start(bf16[896,1280]{1,0:T(8,128)(2,1)} %param.22), channel_id=1, source_target_pairs={{0,16},{8,24},{16,0},{24,8},{1,17},{9,25},{17,1},{25,9},{2,18},{10... | collective-permute-start | bytes 6881288 | tf_op jit(solution)/shard_map/ppermute | solution.py:49
  106.7 99.0 %collective-permute-start.6 = (bf16[896,1280]{1,0:T(8,128)(2,1)}, bf16[896,1280]{1,0:T(8,128)(2,1)S(1)}, u32[]{:S(2)}, u32[]{:S(2)}) collective-permute-start(bf16[896,1280]{1,0:T(8,128)(2,1)} %param.21), channel_id=1, source_target_pairs={{0,16},{8,24},{16,0},{24,8},{1,17},{9,25},{17,1},{25,9},{2,18},{10... | collective-permute-start | bytes 6881288 | tf_op jit(solution)/shard_map/ppermute | solution.py:49
  158.1 5.1 copy-start.14
  158.1 47.5 %copy-start.10 = (bf16[896,1280]{1,0:T(8,128)(2,1)S(1)}, bf16[896,1280]{1,0:T(8,128)(2,1)}, u32[]{:S(2)}) copy-start(bf16[896,1280]{1,0:T(8,128)(2,1)} %param.21) | copy-start | bytes 6881284
  163.2 53.3 %collective-permute-start.9 = (bf16[2,896,1280]{2,1,0:T(8,128)(2,1)}, bf16[2,896,1280]{2,1,0:T(8,128)(2,1)}, u32[]{:S(2)}, u32[]{:S(2)}) collective-permute-start(bf16[2,896,1280]{2,1,0:T(8,128)(2,1)} %pad_maximum_fusion.4), channel_id=1, source_target_pairs={{0,8},{8,0},{16,24},{24,16},{1,9},{9,1},{17,25},{25,17},{2,10},{10... | collective-permute-start | bytes 13762568 | tf_op jit(solution)/shard_map/ppermute | solution.py:52
  205.6 4.5 copy-start.19
  205.6 6.7 copy-start.18
  208.4 18.3 %collective-permute-start.7 = (bf16[2,896,1280]{2,1,0:T(8,128)(2,1)}, bf16[2,896,1280]{2,1,0:T(8,128)(2,1)}, u32[]{:S(2)}, u32[]{:S(2)}) collective-permute-start(bf16[2,896,1280]{2,1,0:T(8,128)(2,1)} %pad_maximum_fusion.3), channel_id=1, source_target_pairs={{0,8},{8,0},{16,24},{24,16},{1,9},{9,1},{17,25},{25,17},{2,10},{10... | collective-permute-start | bytes 13762568 | tf_op jit(solution)/shard_map/ppermute | solution.py:52
  208.5 3.9 collective-permute-start.12
  210.1 3.5 collective-permute-start
  213.7 2.5 collective-permute-start.1
  216.6 10.2 copy-start.11
  216.6 10.2 copy-start.13
  956.8 11.3 %copy-start.1 = (bf16[768,3584]{1,0:T(8,128)(2,1)S(1)}, bf16[768,3584]{1,0:T(8,128)(2,1)}, u32[]{:S(2)}) copy-start(bf16[768,3584]{1,0:T(8,128)(2,1)} %reduce_sum.74) | copy-start | bytes 16515076
  956.8 11.3 %copy-start.3 = (bf16[768,896]{1,0:T(8,128)(2,1)S(1)}, bf16[768,896]{1,0:T(8,128)(2,1)}, u32[]{:S(2)}) copy-start(bf16[768,896]{1,0:T(8,128)(2,1)} %copy-done.2) | copy-start | bytes 4128772
  956.8 11.3 %copy-start.5 = (bf16[768,896]{1,0:T(8,128)(2,1)S(1)}, bf16[768,896]{1,0:T(8,128)(2,1)}, u32[]{:S(2)}) copy-start(bf16[768,896]{1,0:T(8,128)(2,1)} %copy-done.4) | copy-start | bytes 4128772
  956.8 11.3 %copy-start.7 = (bf16[768,896]{1,0:T(8,128)(2,1)S(1)}, bf16[768,896]{1,0:T(8,128)(2,1)}, u32[]{:S(2)}) copy-start(bf16[768,896]{1,0:T(8,128)(2,1)} %copy-done.6) | copy-start | bytes 4128772
  956.8 11.3 %copy-start.9 = (bf16[768,896]{1,0:T(8,128)(2,1)S(1)}, bf16[768,896]{1,0:T(8,128)(2,1)}, u32[]{:S(2)}) copy-start(bf16[768,896]{1,0:T(8,128)(2,1)} %copy-done.8) | copy-start | bytes 4128772
  996.2 4.5 collective-permute-start.10
  1000.7 2.6 collective-permute-start.11
  1007.5 32.3 %all-to-all-start.1 = ((f32[32,16,448]{2,1,0:T(8,128)}), f32[32,16,448]{2,1,0:T(8,128)S(1)}, u32[]{:S(2)}, u32[]{:S(2)}) async-start(f32[32,16,448]{2,1,0:T(8,128)} %bitcast.109), calls=%async_computation.1 | async-start | bytes 2097152 | tf_op jit(solution)/shard_map/all_to_all | solution.py:201
  1012.2 1.2 collective-permute-start.13
  (6 other events, 18.5 us)
Sparse Core Ops, SparseCore 0:
  105.2 833.4 all-gather.2
